TPU v7x, 256 devices: a whole 4x4x8 slice. The times are simulated.
256 devices in a mesh: dp: 32 (over z, x), tensor: 8 (over y, core).
Axes of the slice: x: 4, y: 4, z: 8, core: 2. Of those that a mesh axis runs over, the one named last changes fastest.
Arguments:
- gradients: float32 [32, 2368, 1024], P('dp', None, 'tensor'), may hold values from -96 to 96
- weights: float32 [2368, 1024], P(None, 'tensor'), may hold values from -64 to 64
- first_moment: float32 [2368, 1024], P(None, 'tensor'), may hold values from -64 to 64
- second_moment: float32 [2368, 1024], P(None, 'tensor'), may hold values from 0.05 to 2
Outputs:
- weights_new: float32 [2368, 1024], P(None, 'tensor')
- first_new: float32 [2368, 1024], P(None, 'tensor')
- second_new: float32 [2368, 1024], P(None, 'tensor')
- copies: bfloat16 [2368, 1024], replicated
- ratios: float32 [4], replicated
All inputs are finite; a program needn't handle non-finite values.
Results may differ from a plain program's by a relative error of at most 0.0004.
Values may be sent and summed in bfloat16 or wider, within the bound.
No kernel may reach another device: no remote copies, remote signals or barrier semaphores. Data moves between devices by JAX's collectives and lax.ppermute only.
A program may use at most 64 MiB of HBM per device.

v0:
```python
import jax
import jax.numpy as jnp
import numpy as np
from jax import lax
from jax.sharding import Mesh
from jax.sharding import PartitionSpec as P

D = 1024
HID = 1342
beta_one = 0.9
beta_two = 0.999
correct_one = 1.0 - 0.9**20
correct_two = 1.0 - 0.999**20
epsilon = 1e-06
learn_rate = 0.01
decay_rate = 0.01
DP = ("z", "x")
TN = ("y", "core")


def group_table(row_count):
    row_ids = lax.broadcasted_iota(jnp.int32, (row_count, 4), 0)
    which = lax.broadcasted_iota(jnp.int32, (row_count, 4), 1)
    group = jnp.where(row_ids < D, 0, jnp.where(row_ids < D + HID, 1, row_ids - D - HID + 2))
    return (group == which).astype(jnp.float32)


def group_squares(values, seg_table):
    row_sums = jnp.sum(values * values, axis=1)
    return jnp.dot(row_sums, seg_table, precision=lax.Precision.HIGHEST)


def adam_part(grad, weights, first_moment, second_moment, seg_table):
    first_new = beta_one * first_moment + (1.0 - beta_one) * grad
    second_new = beta_two * second_moment + (1.0 - beta_two) * grad * grad
    decay = decay_rate * (seg_table[:, 0] + seg_table[:, 1])
    update = (
        first_new / correct_one / (jnp.sqrt(second_new / correct_two) + epsilon)
        + decay[:, None] * weights
    )
    return (first_new, second_new, update)


def apply_ratios(weights, update, seg_table, weight_total, step_total):
    ratios = jnp.sqrt(weight_total) / jnp.sqrt(step_total)
    row_ratio = jnp.dot(seg_table, ratios, precision=lax.Precision.HIGHEST)
    return (weights - learn_rate * row_ratio[:, None] * update, ratios)


def dp_sum(x, nz, nx):
    rows, cols = x.shape
    unit = 8 * nz * nx
    padded = -(-rows // unit) * unit
    y = jnp.pad(x, ((0, padded - rows), (0, 0)))
    y = lax.all_to_all(y.reshape(nx, padded // nx, cols), "x", 0, 0, tiled=False).sum(0)
    y = lax.all_to_all(y.reshape(nz, padded // (nx * nz), cols), "z", 0, 0, tiled=False).sum(0)
    y = lax.all_to_all(jnp.broadcast_to(y[None], (nz,) + y.shape), "z", 0, 0, tiled=False)
    y = y.reshape(padded // nx, cols)
    y = lax.all_to_all(jnp.broadcast_to(y[None], (nx,) + y.shape), "x", 0, 0, tiled=False)
    return y.reshape(padded, cols)[:rows]


def tensor_sum(v, ny, ncore):
    for axis, size in (("core", ncore), ("y", ny)):
        step = 1
        while step < size:
            v = v + lax.ppermute(v, axis, [(i, i ^ step) for i in range(size)])
            step *= 2
    return v


def make_shards(nz, nx, ny, ncore):

    def shards(gradients, weights, first_moment, second_moment):
        local_grad = gradients[0]
        row_count = weights.shape[0]
        seg_table = group_table(row_count)
        grad = dp_sum(local_grad, nz, nx) / (nz * nx)
        first_new, second_new, update = adam_part(
            grad, weights, first_moment, second_moment, seg_table
        )
        both = jnp.concatenate(
            [group_squares(weights, seg_table), group_squares(update, seg_table)]
        )
        both = tensor_sum(both, ny, ncore)
        weight_total, step_total = (both[:4], both[4:])
        weights_new, ratios = apply_ratios(weights, update, seg_table, weight_total, step_total)
        copies = lax.all_gather(weights_new.astype(jnp.bfloat16), TN, axis=1, tiled=True)
        return (weights_new, first_new, second_new, copies, ratios)

    return shards


def physical_mesh(mesh):
    devices = mesh.devices
    dp_devices = devices[:, 0]
    nx = len({d.coords[0] for d in dp_devices})
    nz = dp_devices.size // nx
    tn_devices = devices[0, :]
    ncore = len({d.core_on_chip for d in tn_devices})
    ny = tn_devices.size // ncore
    return (Mesh(devices.reshape(nz, nx, ny, ncore), ("z", "x", "y", "core")), (nz, nx, ny, ncore))


def solution(mesh):
    mesh2, sizes = physical_mesh(mesh)
    return jax.shard_map(
        make_shards(*sizes),
        mesh=mesh2,
        in_specs=(P(DP, None, TN), P(None, TN), P(None, TN), P(None, TN)),
        out_specs=(P(None, TN), P(None, TN), P(None, TN), P(), P()),
        check_vma=False,
    )
```

profile of v0, /device:TPU:1, one launch (start us, length us, event | category | flops | bytes accessed | tf_op | source)
XLA Modules:
  0.0 149.0 jit_solution(8851995358770724701)
XLA Ops:
  7.2 1.4 pad.4
  8.5 21.6 %all_to_all.20 = f32[4,640,128]{2,1,0:T(8,128)S(1)} all-to-all(f32[4,640,128]{2,1,0:T(8,128)S(1)} %bitcast.17), channel_id=1, replica_groups=mesh['z'=8,'x'=4,'y'=4,'core'=2] {'x'}, dimensions={0} | all-to-all | bytes 2621440 | tf_op jit(solution)/shard_map/all_to_all | solution.py:55
  30.2 0.1 reduce_sum.37
  30.3 18.7 %all_to_all.21 = f32[8,80,128]{2,1,0:T(8,128)S(1)} all-to-all(f32[8,80,128]{2,1,0:T(8,128)S(1)} %bitcast.19), channel_id=1, replica_groups=mesh['z'=8,'x'=4,'y'=4,'core'=2] {'z'}, dimensions={0} | all-to-all | bytes 655360 | tf_op jit(solution)/shard_map/all_to_all | solution.py:56
  49.0 12.8 %all_to_all.22 = f32[8,80,128]{2,1,0:T(8,128)S(1)} all-to-all(f32[8,80,128]{2,1,0:T(8,128)S(1)} %broadcast_in_dim.24), channel_id=1, replica_groups=mesh['z'=8,'x'=4,'y'=4,'core'=2] {'z'}, dimensions={0} | all-to-all | bytes 655360 | tf_op jit(solution)/shard_map/all_to_all | solution.py:57
  61.8 1.1 broadcast_in_dim.26
  62.9 3.7 %all-to-all-start.3 = ((f32[4,640,128]{2,1,0:T(8,128)}), f32[4,640,128]{2,1,0:T(8,128)S(1)}, u32[]{:S(2)}, u32[]{:S(2)}) async-start(f32[4,640,128]{2,1,0:T(8,128)} %broadcast_in_dim.26), calls=%async_computation.3 | async-start | bytes 2621440 | tf_op jit(solution)/shard_map/all_to_all | solution.py:59
  66.8 13.2 %all-to-all-done.3 = f32[4,640,128]{2,1,0:T(8,128)S(1)} async-done(((f32[4,640,128]{2,1,0:T(8,128)}), f32[4,640,128]{2,1,0:T(8,128)S(1)}, u32[]{:S(2)}, u32[]{:S(2)}) %all-to-all-start.3) | async-done | bytes 1310752 | tf_op jit(solution)/shard_map/all_to_all | solution.py:59
  79.9 4.0 %multiply_reduce_fusion = (f32[2368]{0:T(1024)S(1)}, f32[2368,128]{1,0:T(8,128)S(1)}, f32[2368,128]{1,0:T(8,128)}, f32[2368,128]{1,0:T(8,128)}, f32[2368]{0:T(1024)S(1)}) fusion(f32[2368,128]{1,0:T(8,128)S(1)} %copy-done, f32[2368]{0:T(1024)S(1)} %fusion.1, f32[2560,128]{1,0:T(8,128)S(1)} %bitcast.18, f32[2368,128]{1,0:T(8,128)} %param.6, f32[2368,128]{1,0:T(8,128)} %param.7), kind=kLoop, calls=%fused_computation.1 | loop fusion | flops 5451136 | bytes 8515328 | tf_op jit(solution)/shard_map/reduce_sum | solution.py:29
  83.9 0.1 convolution_bitcast_fusion
  84.1 0.2 convolution_bitcast_fusion.1
  84.3 0.1 pad_maximum_fusion
  84.4 5.5 %collective-permute-start = (f32[8]{0:T(128)S(1)}, f32[8]{0:T(128)S(1)}, u32[]{:S(2)}, u32[]{:S(2)}) collective-permute-start(f32[8]{0:T(128)S(1)} %pad_maximum_fusion), channel_id=1, source_target_pairs={{0,1},{1,0},{2,3},{3,2},{4,5},{5,4},{6,7},{7,6},{8,9},{9,8},{10,11... | collective-permute-start | bytes 104 | tf_op jit(solution)/shard_map/ppermute | solution.py:67
  89.9 0.8 collective-permute-done
  90.7 0.1 fusion.10
  90.8 1.3 collective-permute-start.1
  92.1 1.1 collective-permute-done.1
  93.3 2.9 %collective-permute-start.2 = (f32[8]{0:T(128)S(1)}, f32[8]{0:T(128)S(1)}, u32[]{:S(2)}, u32[]{:S(2)}) collective-permute-start(f32[8]{0:T(128)S(1)} %add.59), channel_id=1, source_target_pairs={{0,4},{2,6},{4,0},{6,2},{1,5},{3,7},{5,1},{7,3},{8,12},{10,14},{12... | collective-permute-start | bytes 104 | tf_op jit(solution)/shard_map/ppermute | solution.py:67
  96.2 1.0 collective-permute-done.2
  97.2 0.1 rsqrt_multiply_fusion
  97.3 0.2 convolution_reduce_fusion
  97.5 1.6 %fusion.3 = (bf16[2368,128]{1,0:T(8,128)(2,1)}, f32[2368,128]{1,0:T(8,128)}) fusion(f32[2368,128]{1,0:T(8,128)S(1)} %copy-done, f32[2368,128]{1,0:T(8,128)S(1)} %get-tuple-element.8, f32[2368]{0:T(1024)S(1)} %broadcast_multiply_fusion), kind=kLoop, calls=%fused_computation.20 | loop fusion | flops 909312 | bytes 4252928 | tf_op jit(solution)/shard_map/convert_element_type | solution.py:88
  99.1 38.0 %all-gather.2.cloned.1.call-done = bf16[2368,1024]{1,0:T(8,128)(2,1)} async-done(((bf16[2368,128]{1,0:T(8,128)(2,1)}), bf16[2368,1024]{1,0:T(8,128)(2,1)}) %all-gather.2.cloned.1.call-update) | async-done | bytes 4849680 | tf_op jit(solution)/shard_map/all_gather | solution.py:88
  137.1 5.1 %copy.10 = bf16[2368,1024]{1,0:T(8,128)(2,1)} copy(bf16[2368,1024]{1,0:T(8,128)(2,1)} %all-gather.2.cloned.1.call-done) | data formatting | bytes 9699328
  (17 shorter events, 0.2 us)
Async XLA Ops:
  62.9 17.0 %copy-start = (f32[2368,128]{1,0:T(8,128)S(1)}, f32[2368,128]{1,0:T(8,128)}, u32[]{:S(2)}) copy-start(f32[2368,128]{1,0:T(8,128)} %param.5) | copy-start | bytes 3637252
  62.9 17.0 %all-to-all-start.3 = ((f32[4,640,128]{2,1,0:T(8,128)}), f32[4,640,128]{2,1,0:T(8,128)S(1)}, u32[]{:S(2)}, u32[]{:S(2)}) async-start(f32[4,640,128]{2,1,0:T(8,128)} %broadcast_in_dim.26), calls=%async_computation.3 | async-start | bytes 2621440 | tf_op jit(solution)/shard_map/all_to_all | solution.py:59
  66.6 70.5 %all-gather.2.cloned.1.call-start = ((), (), s32[]{:S(2)}) async-start(), calls=%async_computation.4 | async-start | bytes 5455872 | tf_op jit(solution)/shard_map/all_gather | solution.py:88
  84.4 6.4 %collective-permute-start = (f32[8]{0:T(128)S(1)}, f32[8]{0:T(128)S(1)}, u32[]{:S(2)}, u32[]{:S(2)}) collective-permute-start(f32[8]{0:T(128)S(1)} %pad_maximum_fusion), channel_id=1, source_target_pairs={{0,1},{1,0},{2,3},{3,2},{4,5},{5,4},{6,7},{7,6},{8,9},{9,8},{10,11... | collective-permute-start | bytes 104 | tf_op jit(solution)/shard_map/ppermute | solution.py:67
  90.8 2.4 %collective-permute-start.1 = (f32[8]{0:T(128)S(1)}, f32[8]{0:T(128)S(1)}, u32[]{:S(2)}, u32[]{:S(2)}) collective-permute-start(f32[8]{0:T(128)S(1)} %fusion.10), channel_id=1, source_target_pairs={{0,2},{2,0},{4,6},{6,4},{1,3},{3,1},{5,7},{7,5},{8,10},{10,8},{12,... | collective-permute-start | bytes 104 | tf_op jit(solution)/shard_map/ppermute | solution.py:67
  93.3 3.9 %collective-permute-start.2 = (f32[8]{0:T(128)S(1)}, f32[8]{0:T(128)S(1)}, u32[]{:S(2)}, u32[]{:S(2)}) collective-permute-start(f32[8]{0:T(128)S(1)} %add.59), channel_id=1, source_target_pairs={{0,4},{2,6},{4,0},{6,2},{1,5},{3,7},{5,1},{7,3},{8,12},{10,14},{12... | collective-permute-start | bytes 104 | tf_op jit(solution)/shard_map/ppermute | solution.py:67
  97.3 1.8 %copy-start.1 = (f32[4]{0:T(128)}, f32[4]{0:T(128)S(1)}, u32[]{:S(2)}) copy-start(f32[4]{0:T(128)S(1)} %rsqrt_multiply_fusion) | copy-start | bytes 52
Sparse Core Ops, SparseCore 0:
  99.2 37.7 all-gather.1
where the time goes:
time: 149 us
  waiting for transfers between devices  54.1 us (36%)
  blocking collectives  53.1 us (36%)
  between operations  14.1 us (9%)
  starting transfers between devices  13.5 us (9%)
  local copies, waits for them, and re-layouts  7.68 us (5%)
  other arithmetic  6.06 us (4%)
    all_gather x1, waiting for transfers between devices, shards(): lax.all_gather(weights_new.astype(jnp.bfloat16), TN, axis=1, tiled=True)  38 us
    all_to_all x1, blocking collectives, dp_sum(): lax.all_to_all(y.reshape(nx, padded // nx, cols), 'x', 0, 0, tiled=False)  21.6 us
    all_to_all x1, blocking collectives, dp_sum(): lax.all_to_all(y.reshape(nz, padded // (nx * nz), cols), 'z', 0, 0, tiled...  18.7 us
    all_to_all x1, waiting for transfers between devices, dp_sum(): lax.all_to_all(jnp.broadcast_to(y[None], (nx,) + y.shape), 'x', 0, 0, til...  13.2 us
    all_to_all x1, blocking collectives, dp_sum(): lax.all_to_all(jnp.broadcast_to(y[None], (nz,) + y.shape), 'z', 0, 0, til...  12.8 us
    ppermute x3, starting transfers between devices, tensor_sum(): v = v + lax.ppermute(v, axis, [(i, i ^ step) for i in range(size)])  9.76 us
    unnamed x5, local copies, waits for them, and re-layouts  5.13 us
    reduce_sum x1, other arithmetic, group_squares(): row_sums = jnp.sum(values * values, axis=1)  3.96 us
  transfers between devices with their start and end apart: 5, of which 5 were waited for; matrix products, arithmetic and copies ran while one was open for 0% of the time, Pallas kernels for 0%

commit v1 on v0

--- a/solution.py
+++ b/solution.py
@@ -85,7 +85,16 @@
         both = tensor_sum(both, ny, ncore)
         weight_total, step_total = (both[:4], both[4:])
         weights_new, ratios = apply_ratios(weights, update, seg_table, weight_total, step_total)
-        copies = lax.all_gather(weights_new.astype(jnp.bfloat16), TN, axis=1, tiled=True)
+
+        def test_steps_all(arr_in):
+            return jnp.concatenate(
+                lax.all_to_all(
+                    jnp.stack([arr_in for _ in range(lax.psum(1, TN))], axis=0), TN, 0, 0
+                ),
+                axis=1,
+            )
+
+        copies = test_steps_all(weights_new.astype(jnp.bfloat16))
         return (weights_new, first_new, second_new, copies, ratios)
 
     return shards

time: 149 us -> 171 us (1.15)
  blocking collectives: 53.1 us -> 116 us
  waiting for transfers between devices: 54.1 us -> 16.2 us
  between operations: 14.1 us -> 0.73 us
  local copies, waits for them, and re-layouts: 7.68 us -> 18.1 us
    all_to_all x0 -> x1, blocking collectives: none -> 62.9 us  [test_steps_all(): lax.all_to_all(jnp.stack([arr_in for _ in range(lax.psum(1, TN))], axis=0...]
    all_gather x1 -> x0, waiting for transfers between devices: 38 us -> none  [shards(): lax.all_gather(weights_new.astype(jnp.bfloat16), TN, axis=1, tiled=True)]
    reshape x0 -> x1, local copies, waits for them, and re-layouts: none -> 7.41 us  [test_steps_all(): jnp.concatenate(lax.all_to_all(jnp.stack([arr_in for _ in range(lax.psum(...]
    unnamed x5, local copies, waits for them, and re-layouts: 5.13 us -> 7.52 us
  transfers between devices with their start and end apart: 5 -> 4, of which waited for: 5 -> 4; matrix products, arithmetic and copies ran while one was open for 0% -> 0% of each run, Pallas kernels for 0% -> 0%
where the time goes in v1:
time: 171 us
  blocking collectives  116 us (68%)
  local copies, waits for them, and re-layouts  18.1 us (11%)
  waiting for transfers between devices  16.2 us (9%)
  starting transfers between devices  13.4 us (8%)
  other arithmetic  5.86 us (3%)
    all_to_all x1, blocking collectives, test_steps_all(): lax.all_to_all(jnp.stack([arr_in for _ in range(lax.psum(1, TN))], axis=0...  62.9 us
    all_to_all x1, blocking collectives, dp_sum(): lax.all_to_all(y.reshape(nx, padded // nx, cols), 'x', 0, 0, tiled=False)  21.6 us
    all_to_all x1, blocking collectives, dp_sum(): lax.all_to_all(y.reshape(nz, padded // (nx * nz), cols), 'z', 0, 0, tiled...  18.7 us
    all_to_all x1, waiting for transfers between devices, dp_sum(): lax.all_to_all(jnp.broadcast_to(y[None], (nx,) + y.shape), 'x', 0, 0, til...  13.2 us
    all_to_all x1, blocking collectives, dp_sum(): lax.all_to_all(jnp.broadcast_to(y[None], (nz,) + y.shape), 'z', 0, 0, til...  12.8 us
    ppermute x3, starting transfers between devices, tensor_sum(): v = v + lax.ppermute(v, axis, [(i, i ^ step) for i in range(size)])  9.76 us
    unnamed x5, local copies, waits for them, and re-layouts  7.52 us
    reshape x1, local copies, waits for them, and re-layouts, test_steps_all(): jnp.concatenate(lax.all_to_all(jnp.stack([arr_in for _ in range(lax.psum(...  7.41 us
  transfers between devices with their start and end apart: 4, of which 4 were waited for; matrix products, arithmetic and copies ran while one was open for 0% of the time, Pallas kernels for 0%

profile of v1, /device:TPU:1, one launch (start us, length us, event | category | flops | bytes accessed | tf_op | source)
XLA Modules:
  0.0 170.8 jit_solution(8291064784099711477)
XLA Ops:
  0.6 1.4 pad.4
  2.0 21.6 %all_to_all.25 = f32[4,640,128]{2,1,0:T(8,128)S(1)} all-to-all(f32[4,640,128]{2,1,0:T(8,128)S(1)} %bitcast.21), channel_id=1, replica_groups=mesh['z'=8,'x'=4,'y'=4,'core'=2] {'x'}, dimensions={0} | all-to-all | bytes 2621440 | tf_op jit(solution)/shard_map/all_to_all | solution.py:55
  23.6 0.1 reduce_sum.37
  23.7 18.7 %all_to_all.26 = f32[8,80,128]{2,1,0:T(8,128)S(1)} all-to-all(f32[8,80,128]{2,1,0:T(8,128)S(1)} %bitcast.23), channel_id=1, replica_groups=mesh['z'=8,'x'=4,'y'=4,'core'=2] {'z'}, dimensions={0} | all-to-all | bytes 655360 | tf_op jit(solution)/shard_map/all_to_all | solution.py:56
  42.4 12.8 %all_to_all.27 = f32[8,80,128]{2,1,0:T(8,128)S(1)} all-to-all(f32[8,80,128]{2,1,0:T(8,128)S(1)} %broadcast_in_dim.24), channel_id=1, replica_groups=mesh['z'=8,'x'=4,'y'=4,'core'=2] {'z'}, dimensions={0} | all-to-all | bytes 655360 | tf_op jit(solution)/shard_map/all_to_all | solution.py:57
  55.3 1.1 broadcast_in_dim.26
  56.4 3.7 %all-to-all-start.3 = ((f32[4,640,128]{2,1,0:T(8,128)}), f32[4,640,128]{2,1,0:T(8,128)S(1)}, u32[]{:S(2)}, u32[]{:S(2)}) async-start(f32[4,640,128]{2,1,0:T(8,128)} %broadcast_in_dim.26), calls=%async_computation.3 | async-start | bytes 2621440 | tf_op jit(solution)/shard_map/all_to_all | solution.py:59
  60.2 13.2 %all-to-all-done.3 = f32[4,640,128]{2,1,0:T(8,128)S(1)} async-done(((f32[4,640,128]{2,1,0:T(8,128)}), f32[4,640,128]{2,1,0:T(8,128)S(1)}, u32[]{:S(2)}, u32[]{:S(2)}) %all-to-all-start.3) | async-done | bytes 1310752 | tf_op jit(solution)/shard_map/all_to_all | solution.py:59
  73.4 4.0 %multiply_reduce_fusion = (f32[2368]{0:T(1024)S(1)}, f32[2368,128]{1,0:T(8,128)S(1)}, f32[2368,128]{1,0:T(8,128)}, f32[2368,128]{1,0:T(8,128)}, f32[2368]{0:T(1024)S(1)}) fusion(f32[2368,128]{1,0:T(8,128)S(1)} %copy-done, f32[2368]{0:T(1024)S(1)} %fusion.1, f32[2560,128]{1,0:T(8,128)S(1)} %bitcast.22, f32[2368,128]{1,0:T(8,128)} %param.6, f32[2368,128]{1,0:T(8,128)} %param.7), kind=kLoop, calls=%fused_computation.1 | loop fusion | flops 5451136 | bytes 8515328 | tf_op jit(solution)/shard_map/reduce_sum | solution.py:29
  77.4 0.1 convolution_bitcast_fusion
  77.5 0.2 convolution_bitcast_fusion.1
  77.7 0.1 pad_maximum_fusion
  77.9 5.5 %collective-permute-start = (f32[8]{0:T(128)S(1)}, f32[8]{0:T(128)S(1)}, u32[]{:S(2)}, u32[]{:S(2)}) collective-permute-start(f32[8]{0:T(128)S(1)} %pad_maximum_fusion), channel_id=1, source_target_pairs={{0,1},{1,0},{2,3},{3,2},{4,5},{5,4},{6,7},{7,6},{8,9},{9,8},{10,11... | collective-permute-start | bytes 104 | tf_op jit(solution)/shard_map/ppermute | solution.py:67
  83.4 0.8 collective-permute-done
  84.3 1.3 collective-permute-start.1
  85.6 1.1 collective-permute-done.1
  86.7 2.9 %collective-permute-start.2 = (f32[8]{0:T(128)S(1)}, f32[8]{0:T(128)S(1)}, u32[]{:S(2)}, u32[]{:S(2)}) collective-permute-start(f32[8]{0:T(128)S(1)} %add.59), channel_id=1, source_target_pairs={{0,4},{2,6},{4,0},{6,2},{1,5},{3,7},{5,1},{7,3},{8,12},{10,14},{12... | collective-permute-start | bytes 104 | tf_op jit(solution)/shard_map/ppermute | solution.py:67
  89.6 1.0 collective-permute-done.2
  90.7 0.2 convolution_reduce_fusion
  90.9 1.4 fusion.3
  92.4 0.6 stack.2
  93.0 62.9 %all_to_all.28 = bf16[8,2368,128]{2,1,0:T(8,128)(2,1)} all-to-all(bf16[8,2368,128]{2,1,0:T(8,128)(2,1)S(1)} %stack.2), channel_id=1, replica_groups=mesh['z'=8,'x'=4,'y'=4,'core'=2] {'y','core'}, dimensions={0} | all-to-all | bytes 9699328 | tf_op jit(solution)/shard_map/all_to_all | solution.py:91
  155.8 7.4 %copy.11 = bf16[2368,8,128]{0,2,1:T(8,128)(2,1)} copy(bf16[2368,8,128]{2,0,1:T(8,128)(2,1)} %bitcast.20) | data formatting | bytes 9699328 | tf_op jit(solution)/shard_map/reshape | solution.py:90
  163.3 7.5 %copy.12 = bf16[2368,1024]{1,0:T(8,128)(2,1)} copy(bf16[2368,1024]{0,1:T(8,128)(2,1)} %bitcast.19) | data formatting | bytes 9699328
  (17 shorter events, 0.3 us)
Async XLA Ops:
  56.4 17.0 %copy-start = (f32[2368,128]{1,0:T(8,128)S(1)}, f32[2368,128]{1,0:T(8,128)}, u32[]{:S(2)}) copy-start(f32[2368,128]{1,0:T(8,128)} %param.5) | copy-start | bytes 3637252
  56.4 17.0 %all-to-all-start.3 = ((f32[4,640,128]{2,1,0:T(8,128)}), f32[4,640,128]{2,1,0:T(8,128)S(1)}, u32[]{:S(2)}, u32[]{:S(2)}) async-start(f32[4,640,128]{2,1,0:T(8,128)} %broadcast_in_dim.26), calls=%async_computation.3 | async-start | bytes 2621440 | tf_op jit(solution)/shard_map/all_to_all | solution.py:59
  77.9 6.4 %collective-permute-start = (f32[8]{0:T(128)S(1)}, f32[8]{0:T(128)S(1)}, u32[]{:S(2)}, u32[]{:S(2)}) collective-permute-start(f32[8]{0:T(128)S(1)} %pad_maximum_fusion), channel_id=1, source_target_pairs={{0,1},{1,0},{2,3},{3,2},{4,5},{5,4},{6,7},{7,6},{8,9},{9,8},{10,11... | collective-permute-start | bytes 104 | tf_op jit(solution)/shard_map/ppermute | solution.py:67
  84.3 2.4 %collective-permute-start.1 = (f32[8]{0:T(128)S(1)}, f32[8]{0:T(128)S(1)}, u32[]{:S(2)}, u32[]{:S(2)}) collective-permute-start(f32[8]{0:T(128)S(1)} %fusion.10), channel_id=1, source_target_pairs={{0,2},{2,0},{4,6},{6,4},{1,3},{3,1},{5,7},{7,5},{8,10},{10,8},{12,... | collective-permute-start | bytes 104 | tf_op jit(solution)/shard_map/ppermute | solution.py:67
  86.7 3.9 %collective-permute-start.2 = (f32[8]{0:T(128)S(1)}, f32[8]{0:T(128)S(1)}, u32[]{:S(2)}, u32[]{:S(2)}) collective-permute-start(f32[8]{0:T(128)S(1)} %add.59), channel_id=1, source_target_pairs={{0,4},{2,6},{4,0},{6,2},{1,5},{3,7},{5,1},{7,3},{8,12},{10,14},{12... | collective-permute-start | bytes 104 | tf_op jit(solution)/shard_map/ppermute | solution.py:67
  90.7 1.6 copy-start.1
